TPU v7x, 32 devices: a whole 2x2x4 slice. The times are simulated.
32 devices in a mesh: lvl: 4 (over y, x), prow: 4 (over z), pcol: 2 (over core).
Axes of the slice: x: 2, y: 2, z: 4, core: 2. Of those that a mesh axis runs over, the one named last changes fastest.
Arguments:
- rhs: float32 [4, 2, 1024, 256], P('lvl', 'pcol'), may hold values from -6 to 6
- diag_inverse: bfloat16 [4, 2, 1024, 1024], P('lvl', 'pcol', 'prow'), may hold values from -0.1875 to 0.1875
- off_tiles: bfloat16 [4, 2, 32, 32, 1024], P('lvl', 'pcol', 'prow'), may hold values from -0.625 to 0.625
- panel_super: int32 [4, 2, 8], P('lvl', 'pcol'), may hold values from 0 to 7, as said below
- off_device: int32 [4, 2, 32], P('lvl', 'pcol', 'prow'), may hold values from 0 to 7, as said below
- off_block: int32 [4, 2, 32], P('lvl', 'pcol', 'prow'), may hold values from 0 to 47, as said below
- offdiag_block_panel: int32 [4, 2, 32], P('lvl', 'pcol', 'prow'), may hold values from 0 to 7
Outputs:
- solution: float32 [4, 2, 1024, 256], P('lvl', 'pcol', 'prow')
- outer: float32 [4, 2, 512, 256], P('lvl', 'pcol')
Inputs may be any that keep to these rules, and one draw needn't show every extreme that they name: `panel_super`: within a group ids start at 0 and rise by 0 or 1 from panel to panel; panels of one id form one supernode. `off_device`: one device sends at most 2 block rows to any one target group; some group receives 2 from every device. `off_block`: A block under 1024 / 32 (a window row) goes only to a group on a higher level than the sender's; the others are rows above the window.
All inputs are finite; a program needn't handle non-finite values.
Results may differ from a plain program's by a relative error of at most 0.0055.
Values may be sent and summed in bfloat16 or wider, within the bound.
No kernel may reach another device: no remote copies, remote signals or barrier semaphores. Data moves between devices by JAX's collectives and lax.ppermute only.
A program may use at most 64 MiB of HBM per device.

v0:
```python
import jax
import jax.numpy as jnp
from jax import lax
from jax.sharding import PartitionSpec as P

CAP = 2
ABOVE = 512
NT = 48


def per_device(
    rhs, diag_inverse, off_tiles, panel_super, off_device, off_block, offdiag_block_panel
):
    levels = lax.axis_size("lvl")
    col_groups = lax.axis_size("pcol")
    groups = levels * col_groups
    level_index = lax.axis_index("lvl")
    row_index = lax.axis_index("prow")
    width = rhs.shape[2]
    columns_all = rhs.shape[3]
    row_count = diag_inverse.shape[2]
    tile_count = off_tiles.shape[2]
    block_rows = off_tiles.shape[3]
    panels = panel_super[0, 0]
    panel_cols = width // panels.shape[0]
    col_super = jnp.repeat(panels, panel_cols)
    row_ids = row_index * row_count + jnp.arange(row_count, dtype=jnp.int32)
    row_super = jnp.take(col_super, row_ids)
    inverse = jnp.where(
        row_super[:, None] == col_super[None, :], diag_inverse[0, 0], jnp.zeros((), jnp.bfloat16)
    )
    tile_supernode = jnp.take(panels, offdiag_block_panel[0, 0])
    tiles_used = jnp.where(
        col_super[None, None, :] == tile_supernode[:, None, None],
        off_tiles[0, 0],
        jnp.zeros((), jnp.bfloat16),
    )
    tiles_used = tiles_used.reshape(tile_count * block_rows, width)
    target = off_device[0, 0]
    target_block = off_block[0, 0]
    tile_ids = jnp.arange(tile_count, dtype=jnp.int32)
    earlier = (target[:, None] == target[None, :]) & (tile_ids[:, None] > tile_ids[None, :])
    position = jnp.sum(earlier.astype(jnp.int32), axis=1)
    slot_index = target * CAP + position
    slot_total = groups * CAP
    match = slot_index[None, :] == jnp.arange(slot_total, dtype=jnp.int32)[:, None]
    filled = jnp.any(match, axis=1)
    chosen = jnp.sum(jnp.where(match, tile_ids[None, :], 0), axis=1)
    slot_block = jnp.where(filled, jnp.take(target_block, chosen), -1)
    slot_level = jnp.arange(slot_total, dtype=jnp.int32) // (col_groups * CAP)
    col_blocks = 1
    block_cols = columns_all // col_blocks
    right = rhs[0, 0]
    solved = jnp.zeros((row_count, columns_all), jnp.float32)
    outer = jnp.zeros((ABOVE, columns_all), jnp.float32)
    block_numbers = jnp.arange(NT, dtype=jnp.int32)
    for section in range(levels + col_blocks - 1):
        my_block = section - level_index
        active = (my_block >= 0) & (my_block < col_blocks)
        right_part = right
        solved_rows = jnp.dot(
            inverse, right_part.astype(jnp.bfloat16), preferred_element_type=jnp.float32
        )
        previous = solved
        solved = jnp.where(active, solved_rows, previous)
        updates = jnp.dot(
            tiles_used,
            lax.all_gather(solved_rows.astype(jnp.bfloat16), "prow", axis=0, tiled=True),
            preferred_element_type=jnp.float32,
        )
        updates = updates.astype(jnp.bfloat16).reshape(tile_count, block_rows, block_cols)
        padded = jnp.concatenate(
            [updates, jnp.zeros((1, block_rows, block_cols), jnp.bfloat16)], axis=0
        )
        sending = jnp.take(padded, jnp.where(filled & active, chosen, tile_count), axis=0)
        send_block = jnp.where(active, slot_block, -1)
        incoming_block_rows, received_block = (
            lax.all_to_all(sending, ("lvl", "pcol"), split_axis=0, concat_axis=0, tiled=True),
            lax.all_to_all(send_block, ("lvl", "pcol"), split_axis=0, concat_axis=0, tiled=True),
        )
        from_level = slot_level == section
        choosing_mask = (
            (received_block[:, None] == block_numbers[None, :]) & from_level[:, None]
        ).astype(jnp.bfloat16)
        block_fragments = jnp.einsum(
            "at,apz->tpz", choosing_mask, incoming_block_rows, preferred_element_type=jnp.float32
        )
        summed = block_fragments
        summed = summed.reshape(NT * block_rows, columns_all)
        summed = lax.psum(summed, "prow")
        right = right - summed[:width]
        outer = outer + summed[width:]
    return (solved[None, None], outer[None, None])


def solution(mesh):
    placed = (
        P("lvl", "pcol", None, None),
        P("lvl", "pcol", "prow", None),
        P("lvl", "pcol", "prow", None, None),
        P("lvl", "pcol", None),
        P("lvl", "pcol", "prow"),
        P("lvl", "pcol", "prow"),
        P("lvl", "pcol", "prow"),
    )
    return jax.shard_map(
        per_device,
        mesh=mesh,
        in_specs=placed,
        out_specs=(P("lvl", "pcol", "prow", None), P("lvl", "pcol", None, None)),
        check_vma=False,
    )
```

profile of v0, /device:TPU:0, one launch (start us, length us, event | category | flops | bytes accessed | tf_op | source)
XLA Modules:
  0.0 433.2 jit_solution(8528554265465169059)
XLA Ops:
  7.2 1.0 convert_reduce_fusion
  8.2 0.7 multiply_add_fusion
  8.8 0.1 select_reduce_fusion
  8.9 0.1 fusion.40
  9.1 0.1 reduce_or.12
  9.2 1.3 gather_fusion.1
  10.5 0.1 gather.19
  10.6 0.6 broadcast_select_fusion.4
  11.2 0.6 broadcast_select_fusion.5
  11.8 5.2 %all-to-all-start = ((s32[8,2,1]{1,2,0:T(1,128)}), s32[8,2,1]{1,2,0:T(1,128)S(1)}, u32[]{:S(2)}, u32[]{:S(2)}) async-start(s32[8,2,1]{1,2,0:T(1,128)} %bitcast.9), calls=%async_computation | async-start | bytes 8192 | tf_op jit(solution)/shard_map/all_to_all | solution.py:79
  17.0 0.7 fusion.47
  17.8 0.6 gather_fusion.2
  18.4 0.7 and_select_fusion.4
  19.1 1.4 gather_fusion
  20.6 1.1 fusion.50
  21.7 16.6 %all_gather.12 = bf16[1024,256]{1,0:T(8,128)(2,1)S(1)} all-gather(bf16[256,256]{1,0:T(8,128)(2,1)S(1)} %get-tuple-element.24), channel_id=1, replica_groups=mesh['lvl'=4,'prow'=4,'pcol'=2] {'prow'}, dimensions={0}, use_global_device_ids=true | all-gather | bytes 655360 | tf_op jit(solution)/shard_map/all_gather | solution.py:68
  38.2 0.1 bitcast_select_fusion
  38.3 0.3 convolution_convert_fusion.3
  38.6 0.6 gather_fusion.3
  39.2 0.8 broadcast_select_fusion.3
  40.0 3.8 all-to-all-start.1
  43.9 0.5 broadcast.584
  44.4 0.6 reduce.12
  45.1 5.6 %all-to-all-done.1 = bf16[16,32,256]{2,1,0:T(8,128)(2,1)S(1)} async-done(((bf16[16,32,256]{2,1,0:T(8,128)(2,1)}), bf16[16,32,256]{2,1,0:T(8,128)(2,1)S(1)}, u32[]{:S(2)}, u32[]{:S(2)}) %all-to-all-start.1) | async-done | bytes 262176 | tf_op jit(solution)/shard_map/all_to_all | solution.py:78
  50.7 0.5 fusion.21
  51.2 2.1 copy.31
  53.3 3.3 all-to-all-start.2
  56.6 65.5 %all-reduce.9.cloned.1.call-done = f32[1536,256]{1,0:T(8,128)} async-done(((f32[1536,256]{1,0:T(8,128)}), f32[1536,256]{1,0:T(8,128)}) %all-reduce.9.cloned.1.call-update) | async-done | bytes 1572880 | tf_op jit(solution)/shard_map/psum | solution.py:90
  122.2 2.3 fusion.51
  124.5 15.8 %all_gather.13 = bf16[1024,256]{1,0:T(8,128)(2,1)S(1)} all-gather(bf16[256,256]{1,0:T(8,128)(2,1)S(1)} %get-tuple-element.26), channel_id=1, replica_groups=mesh['lvl'=4,'prow'=4,'pcol'=2] {'prow'}, dimensions={0}, use_global_device_ids=true | all-gather | bytes 655360 | tf_op jit(solution)/shard_map/all_gather | solution.py:68
  140.3 0.3 convolution_convert_fusion.2
  140.7 0.6 gather_fusion.4
  141.2 0.8 broadcast_select_fusion.2
  142.0 3.4 all-to-all-start.3
  145.5 0.6 reduce.13
  146.2 6.1 %all-to-all-done.3 = bf16[16,32,256]{2,1,0:T(8,128)(2,1)S(1)} async-done(((bf16[16,32,256]{2,1,0:T(8,128)(2,1)}), bf16[16,32,256]{2,1,0:T(8,128)(2,1)S(1)}, u32[]{:S(2)}, u32[]{:S(2)}) %all-to-all-start.3) | async-done | bytes 262176 | tf_op jit(solution)/shard_map/all_to_all | solution.py:78
  152.3 0.5 fusion.19
  152.8 2.1 copy.34
  154.9 3.5 all-to-all-start.4
  158.4 63.7 %all-reduce.11.cloned.1.call-done = f32[1536,256]{1,0:T(8,128)} async-done(((f32[1536,256]{1,0:T(8,128)}), f32[1536,256]{1,0:T(8,128)}) %all-reduce.11.cloned.1.call-update) | async-done | bytes 1572880 | tf_op jit(solution)/shard_map/psum | solution.py:90
  222.0 2.6 fusion.52
  224.6 15.8 %all_gather.14 = bf16[1024,256]{1,0:T(8,128)(2,1)S(1)} all-gather(bf16[256,256]{1,0:T(8,128)(2,1)S(1)} %get-tuple-element.28), channel_id=1, replica_groups=mesh['lvl'=4,'prow'=4,'pcol'=2] {'prow'}, dimensions={0}, use_global_device_ids=true | all-gather | bytes 655360 | tf_op jit(solution)/shard_map/all_gather | solution.py:68
  240.5 0.3 convolution_convert_fusion.1
  240.8 1.3 gather_fusion.5
  242.1 1.7 broadcast_select_fusion.1
  243.8 3.4 all-to-all-start.5
  247.3 0.6 reduce.14
  248.0 6.1 %all-to-all-done.5 = bf16[16,32,256]{2,1,0:T(8,128)(2,1)S(1)} async-done(((bf16[16,32,256]{2,1,0:T(8,128)(2,1)}), bf16[16,32,256]{2,1,0:T(8,128)(2,1)S(1)}, u32[]{:S(2)}, u32[]{:S(2)}) %all-to-all-start.5) | async-done | bytes 262176 | tf_op jit(solution)/shard_map/all_to_all | solution.py:78
  254.1 0.5 fusion.17
  254.6 2.1 copy.37
  256.7 3.5 all-to-all-start.6
  260.2 63.7 %all-reduce.13.cloned.1.call-done = f32[1536,256]{1,0:T(8,128)} async-done(((f32[1536,256]{1,0:T(8,128)}), f32[1536,256]{1,0:T(8,128)}) %all-reduce.13.cloned.1.call-update) | async-done | bytes 1572880 | tf_op jit(solution)/shard_map/psum | solution.py:90
  323.8 2.9 fusion.49
  326.8 15.8 %all_gather.15 = bf16[1024,256]{1,0:T(8,128)(2,1)S(1)} all-gather(bf16[256,256]{1,0:T(8,128)(2,1)S(1)} %get-tuple-element.13), channel_id=1, replica_groups=mesh['lvl'=4,'prow'=4,'pcol'=2] {'prow'}, dimensions={0}, use_global_device_ids=true | all-gather | bytes 655360 | tf_op jit(solution)/shard_map/all_gather | solution.py:68
  342.6 0.3 convolution_convert_fusion
  342.9 0.6 gather_fusion.6
  343.5 0.8 broadcast_select_fusion
  344.3 3.4 all-to-all-start.7
  347.8 0.6 reduce.15
  348.5 6.1 %all-to-all-done.7 = bf16[16,32,256]{2,1,0:T(8,128)(2,1)S(1)} async-done(((bf16[16,32,256]{2,1,0:T(8,128)(2,1)}), bf16[16,32,256]{2,1,0:T(8,128)(2,1)S(1)}, u32[]{:S(2)}, u32[]{:S(2)}) %all-to-all-start.7) | async-done | bytes 262176 | tf_op jit(solution)/shard_map/all_to_all | solution.py:78
  354.6 0.5 fusion.15
  355.1 2.1 copy.40
  357.2 67.2 %all-reduce.15.cloned.1.call-done = f32[1536,256]{1,0:T(8,128)} async-done(((f32[1536,256]{1,0:T(8,128)}), f32[1536,256]{1,0:T(8,128)}) %all-reduce.15.cloned.1.call-update) | async-done | bytes 1572880 | tf_op jit(solution)/shard_map/psum | solution.py:90
  424.3 2.3 fusion.6
  (50 shorter events, 1.0 us)
Async XLA Ops:
  7.2 10.5 %copy-start = (s32[1,1,8]{2,1,0:T(1,128)S(1)}, s32[1,1,8]{2,1,0:T(1,128)}, u32[]{:S(2)}) copy-start(s32[1,1,8]{2,1,0:T(1,128)} %param.12) | copy-start | bytes 100
  7.2 13.4 %copy-start.3 = (bf16[1,1,256,1024]{3,2,1,0:T(8,128)(2,1)S(1)}, bf16[1,1,256,1024]{3,2,1,0:T(8,128)(2,1)}, u32[]{:S(2)}) copy-start(bf16[1,1,256,1024]{3,2,1,0:T(8,128)(2,1)} %param.10) | copy-start | bytes 1572868
  7.2 13.4 %copy-start.1 = (f32[1,1,1024,256]{3,2,1,0:T(8,128)S(1)}, f32[1,1,1024,256]{3,2,1,0:T(8,128)}, u32[]{:S(2)}) copy-start(f32[1,1,1024,256]{3,2,1,0:T(8,128)} %param.9) | copy-start | bytes 3145732
  11.8 28.2 %all-to-all-start = ((s32[8,2,1]{1,2,0:T(1,128)}), s32[8,2,1]{1,2,0:T(1,128)S(1)}, u32[]{:S(2)}, u32[]{:S(2)}) async-start(s32[8,2,1]{1,2,0:T(1,128)} %bitcast.9), calls=%async_computation | async-start | bytes 8192 | tf_op jit(solution)/shard_map/all_to_all | solution.py:79
  20.5 17.8 %copy-start.5 = (bf16[1,1,8,32,1024]{4,3,2,1,0:T(8,128)(2,1)S(1)}, bf16[1,1,8,32,1024]{4,3,2,1,0:T(8,128)(2,1)}, u32[]{:S(2)}) copy-start(bf16[1,1,8,32,1024]{4,3,2,1,0:T(8,128)(2,1)} %param.11) | copy-start | bytes 1572868
  40.0 10.7 %all-to-all-start.1 = ((bf16[16,32,256]{2,1,0:T(8,128)(2,1)}), bf16[16,32,256]{2,1,0:T(8,128)(2,1)S(1)}, u32[]{:S(2)}, u32[]{:S(2)}) async-start(bf16[16,32,256]{2,1,0:T(8,128)(2,1)} %broadcast_select_fusion.3), calls=%async_computation.1 | async-start | bytes 524288 | tf_op jit(solution)/shard_map/all_to_all | solution.py:78
  43.8 78.4 %all-reduce.9.cloned.1.call-start = ((), (), s32[]{:S(2)}) async-start(), calls=%async_computation.8 | async-start | bytes 3145728 | tf_op jit(solution)/shard_map/psum | solution.py:90
  53.3 88.7 %all-to-all-start.2 = ((s32[8,2,1]{1,2,0:T(1,128)}), s32[8,2,1]{1,2,0:T(1,128)S(1)}, u32[]{:S(2)}, u32[]{:S(2)}) async-start(s32[8,2,1]{1,2,0:T(1,128)} %bitcast.20), calls=%async_computation.2 | async-start | bytes 8192 | tf_op jit(solution)/shard_map/all_to_all | solution.py:79
  142.0 10.3 %all-to-all-start.3 = ((bf16[16,32,256]{2,1,0:T(8,128)(2,1)}), bf16[16,32,256]{2,1,0:T(8,128)(2,1)S(1)}, u32[]{:S(2)}, u32[]{:S(2)}) async-start(bf16[16,32,256]{2,1,0:T(8,128)(2,1)} %broadcast_select_fusion.2), calls=%async_computation.3 | async-start | bytes 524288 | tf_op jit(solution)/shard_map/all_to_all | solution.py:78
  145.4 76.6 %all-reduce.11.cloned.1.call-start = ((), (), s32[]{:S(2)}) async-start(), calls=%async_computation.9 | async-start | bytes 3145728 | tf_op jit(solution)/shard_map/psum | solution.py:90
  154.9 67.2 %copy-start.2 = (f32[1536,256]{1,0:T(8,128)S(1)}, f32[1536,256]{1,0:T(8,128)}, u32[]{:S(2)}) copy-start(f32[1536,256]{1,0:T(8,128)} %all-reduce.9.cloned.1.call-done) | copy-start | bytes 4718596
  154.9 88.9 %all-to-all-start.4 = ((s32[8,2,1]{1,2,0:T(1,128)}), s32[8,2,1]{1,2,0:T(1,128)S(1)}, u32[]{:S(2)}, u32[]{:S(2)}) async-start(s32[8,2,1]{1,2,0:T(1,128)} %bitcast.24), calls=%async_computation.4 | async-start | bytes 8192 | tf_op jit(solution)/shard_map/all_to_all | solution.py:79
  243.8 10.3 %all-to-all-start.5 = ((bf16[16,32,256]{2,1,0:T(8,128)(2,1)}), bf16[16,32,256]{2,1,0:T(8,128)(2,1)S(1)}, u32[]{:S(2)}, u32[]{:S(2)}) async-start(bf16[16,32,256]{2,1,0:T(8,128)(2,1)} %broadcast_select_fusion.1), calls=%async_computation.5 | async-start | bytes 524288 | tf_op jit(solution)/shard_map/all_to_all | solution.py:78
  247.2 76.6 %all-reduce.13.cloned.1.call-start = ((), (), s32[]{:S(2)}) async-start(), calls=%async_computation.10 | async-start | bytes 3145728 | tf_op jit(solution)/shard_map/psum | solution.py:90
  256.6 67.2 %copy-start.4 = (f32[256,256]{1,0:T(8,128)S(1)}, f32[256,256]{1,0:T(8,128)}, u32[]{:S(2)}) copy-start(f32[256,256]{1,0:T(8,128)} %get-tuple-element.25) | copy-start | bytes 786436
  256.7 87.6 %all-to-all-start.6 = ((s32[8,2,1]{1,2,0:T(1,128)}), s32[8,2,1]{1,2,0:T(1,128)S(1)}, u32[]{:S(2)}, u32[]{:S(2)}) async-start(s32[8,2,1]{1,2,0:T(1,128)} %bitcast.29), calls=%async_computation.6 | async-start | bytes 8192 | tf_op jit(solution)/shard_map/all_to_all | solution.py:79
  344.3 10.3 %all-to-all-start.7 = ((bf16[16,32,256]{2,1,0:T(8,128)(2,1)}), bf16[16,32,256]{2,1,0:T(8,128)(2,1)S(1)}, u32[]{:S(2)}, u32[]{:S(2)}) async-start(bf16[16,32,256]{2,1,0:T(8,128)(2,1)} %broadcast_select_fusion), calls=%async_computation.7 | async-start | bytes 524288 | tf_op jit(solution)/shard_map/all_to_all | solution.py:78
  347.7 76.6 %all-reduce.15.cloned.1.call-start = ((), (), s32[]{:S(2)}) async-start(), calls=%async_computation.11 | async-start | bytes 3145728 | tf_op jit(solution)/shard_map/psum | solution.py:90
Sparse Core Ops, SparseCore 0:
  53.4 68.6 all-reduce.8
  155.0 66.9 all-reduce.10
  256.8 66.9 all-reduce.12
  357.3 66.9 all-reduce.14
where the time goes:
time: 434 us; the launch traced here: 433 us
  waiting for transfers between devices  284 us (65%)
  blocking collectives  64.1 us (15%)
  starting transfers between devices  29.6 us (7%)
  local copies, waits for them, and re-layouts  15.8 us (4%)
  between operations  14.1 us (3%)
  other arithmetic  13.5 us (3%)
  matrix products  12 us (3%)
    psum x4, waiting for transfers between devices, per_device(): summed = lax.psum(summed, 'prow')  260 us
    all_gather x4, blocking collectives, per_device(): lax.all_gather(solved_rows.astype(jnp.bfloat16), 'prow', axis=0, tiled=True)  64.1 us
    all_to_all x4, waiting for transfers between devices, per_device(): lax.all_to_all(sending, ('lvl', 'pcol'), split_axis=0, concat_axis=0, til...  23.9 us
    all_to_all x4, starting transfers between devices, per_device(): lax.all_to_all(send_block, ('lvl', 'pcol'), split_axis=0, concat_axis=0,...  15.4 us
    all_to_all x4, starting transfers between devices, per_device(): lax.all_to_all(sending, ('lvl', 'pcol'), split_axis=0, concat_axis=0, til...  14 us
    dot_general x4, matrix products, per_device(): jnp.dot(inverse, right_part.astype(jnp.bfloat16), preferred_element_type=...  8.92 us
  transfers between devices with their start and end apart: 12, of which 8 were waited for; matrix products, arithmetic and copies ran while one was open for 6% of the time, Pallas kernels for 0%

commit v1 on v0

--- a/solution.py
+++ b/solution.py
@@ -87,7 +87,8 @@
         )
         summed = block_fragments
         summed = summed.reshape(NT * block_rows, columns_all)
-        summed = lax.psum(summed, "prow")
+        parts = lax.all_gather(summed, "prow", axis=0, tiled=False)
+        summed = parts.sum(axis=0)
         right = right - summed[:width]
         outer = outer + summed[width:]
     return (solved[None, None], outer[None, None])

time: 434 us -> 635 us (1.46)
  waiting for transfers between devices: 284 us -> 465 us
  other arithmetic: 13.5 us -> 30.6 us
    all_gather x0 -> x4, waiting for transfers between devices: none -> 441 us  [per_device(): parts = lax.all_gather(summed, 'prow', axis=0, tiled=False)]
    psum x4 -> x0, waiting for transfers between devices: 260 us -> none  [per_device(): summed = lax.psum(summed, 'prow')]
    reduce_sum x0 -> x4, other arithmetic: none -> 16.1 us  [per_device(): summed = parts.sum(axis=0)]
where the time goes in v1:
time: 635 us; the launch traced here: 633 us
  waiting for transfers between devices  465 us (73%)
  blocking collectives  65.3 us (10%)
  other arithmetic  30.6 us (5%)
  starting transfers between devices  29.7 us (5%)
  local copies, waits for them, and re-layouts  16.5 us (3%)
  between operations  14.1 us (2%)
  matrix products  11.8 us (2%)
    all_gather x4, waiting for transfers between devices, per_device(): parts = lax.all_gather(summed, 'prow', axis=0, tiled=False)  441 us
    all_gather x4, blocking collectives, per_device(): lax.all_gather(solved_rows.astype(jnp.bfloat16), 'prow', axis=0, tiled=True)  65.3 us
    all_to_all x4, waiting for transfers between devices, per_device(): lax.all_to_all(sending, ('lvl', 'pcol'), split_axis=0, concat_axis=0, til...  24 us
    reduce_sum x4, other arithmetic, per_device(): summed = parts.sum(axis=0)  16.1 us
    all_to_all x4, starting transfers between devices, per_device(): lax.all_to_all(send_block, ('lvl', 'pcol'), split_axis=0, concat_axis=0,...  14.9 us
    all_to_all x4, starting transfers between devices, per_device(): lax.all_to_all(sending, ('lvl', 'pcol'), split_axis=0, concat_axis=0, til...  14.7 us
  transfers between devices with their start and end apart: 12, of which 8 were waited for; matrix products, arithmetic and copies ran while one was open for 6% of the time, Pallas kernels for 0%

profile of v1, /device:TPU:0, one launch (start us, length us, event | category | flops | bytes accessed | tf_op | source)
XLA Modules:
  0.0 633.5 jit_solution(7282015135312317026)
XLA Ops:
  7.2 1.0 convert_reduce_fusion
  8.2 0.7 multiply_add_fusion
  9.2 1.3 gather_fusion.1
  10.6 0.6 broadcast_select_fusion.4
  11.2 0.6 broadcast_select_fusion.5
  11.8 5.2 all-to-all-start
  17.0 0.7 fusion.47
  17.8 0.6 gather_fusion.2
  18.4 0.7 and_select_fusion.4
  19.1 1.4 gather_fusion
  20.6 1.1 fusion.50
  21.6 16.6 %all_gather.24 = bf16[1024,256]{1,0:T(8,128)(2,1)S(1)} all-gather(bf16[256,256]{1,0:T(8,128)(2,1)S(1)} %get-tuple-element.24), channel_id=1, replica_groups=mesh['lvl'=4,'prow'=4,'pcol'=2] {'prow'}, dimensions={0}, use_global_device_ids=true | all-gather | bytes 655360 | tf_op jit(solution)/shard_map/all_gather | solution.py:68
  38.2 0.1 bitcast_select_fusion
  38.3 0.3 convolution_convert_fusion.3
  38.6 0.6 gather_fusion.3
  39.2 0.8 broadcast_select_fusion.3
  40.0 3.8 all-to-all-start.1
  43.9 0.5 broadcast.584
  44.4 0.6 reduce.12
  45.1 5.6 all-to-all-done.1
  50.7 0.5 fusion.21
  51.2 2.1 copy.31
  53.3 3.2 all-to-all-start.2
  56.5 111.8 %all-gather.5.cloned.1.call-done = f32[4,1536,256]{2,1,0:T(8,128)} async-done(((f32[1,1536,256]{2,1,0:T(8,128)}), f32[4,1536,256]{2,1,0:T(8,128)}) %all-gather.5.cloned.1.call-update) | async-done | bytes 6291472 | tf_op jit(solution)/shard_map/all_gather | solution.py:90
  168.4 3.5 reduce_sum.62
  171.9 2.2 fusion.51
  174.0 16.2 %all_gather.26 = bf16[1024,256]{1,0:T(8,128)(2,1)S(1)} all-gather(bf16[256,256]{1,0:T(8,128)(2,1)S(1)} %get-tuple-element.26), channel_id=1, replica_groups=mesh['lvl'=4,'prow'=4,'pcol'=2] {'prow'}, dimensions={0}, use_global_device_ids=true | all-gather | bytes 655360 | tf_op jit(solution)/shard_map/all_gather | solution.py:68
  190.2 0.3 convolution_convert_fusion.2
  190.6 1.3 gather_fusion.4
  191.8 1.7 broadcast_select_fusion.2
  193.6 3.6 all-to-all-start.3
  197.3 0.7 reduce.13
  198.0 6.1 all-to-all-done.3
  204.2 0.5 fusion.19
  204.6 2.1 copy.34
  206.7 3.3 all-to-all-start.4
  210.0 108.7 %all-gather.7.cloned.1.call-done = f32[4,1536,256]{2,1,0:T(8,128)} async-done(((f32[1,1536,256]{2,1,0:T(8,128)}), f32[4,1536,256]{2,1,0:T(8,128)}) %all-gather.7.cloned.1.call-update) | async-done | bytes 6291472 | tf_op jit(solution)/shard_map/all_gather | solution.py:90
  318.7 4.5 reduce_sum.63
  323.3 2.5 fusion.52
  325.8 16.2 %all_gather.28 = bf16[1024,256]{1,0:T(8,128)(2,1)S(1)} all-gather(bf16[256,256]{1,0:T(8,128)(2,1)S(1)} %get-tuple-element.28), channel_id=1, replica_groups=mesh['lvl'=4,'prow'=4,'pcol'=2] {'prow'}, dimensions={0}, use_global_device_ids=true | all-gather | bytes 655360 | tf_op jit(solution)/shard_map/all_gather | solution.py:68
  342.0 0.3 convolution_convert_fusion.1
  342.4 1.3 gather_fusion.5
  343.6 1.7 broadcast_select_fusion.1
  345.4 3.6 all-to-all-start.5
  349.1 0.7 reduce.14
  349.8 6.1 all-to-all-done.5
  356.0 0.5 fusion.17
  356.4 2.1 copy.37
  358.6 3.3 all-to-all-start.6
  361.9 108.7 %all-gather.9.cloned.1.call-done = f32[4,1536,256]{2,1,0:T(8,128)} async-done(((f32[1,1536,256]{2,1,0:T(8,128)}), f32[4,1536,256]{2,1,0:T(8,128)}) %all-gather.9.cloned.1.call-update) | async-done | bytes 6291472 | tf_op jit(solution)/shard_map/all_gather | solution.py:90
  470.6 4.6 reduce_sum.64
  475.2 2.9 fusion.49
  478.2 16.3 %all_gather.30 = bf16[1024,256]{1,0:T(8,128)(2,1)S(1)} all-gather(bf16[256,256]{1,0:T(8,128)(2,1)S(1)} %get-tuple-element.13), channel_id=1, replica_groups=mesh['lvl'=4,'prow'=4,'pcol'=2] {'prow'}, dimensions={0}, use_global_device_ids=true | all-gather | bytes 655360 | tf_op jit(solution)/shard_map/all_gather | solution.py:68
  494.5 0.3 convolution_convert_fusion
  494.8 0.6 gather_fusion.6
  495.4 0.8 broadcast_select_fusion
  496.2 3.6 all-to-all-start.7
  499.8 0.7 reduce.15
  500.5 6.1 all-to-all-done.7
  506.7 0.5 fusion.15
  507.2 2.1 copy.40
  509.3 112.0 %all-gather.11.cloned.1.call-done = f32[4,1536,256]{2,1,0:T(8,128)} async-done(((f32[1,1536,256]{2,1,0:T(8,128)}), f32[4,1536,256]{2,1,0:T(8,128)}) %all-gather.11.cloned.1.call-update) | async-done | bytes 6291472 | tf_op jit(solution)/shard_map/all_gather | solution.py:90
  621.3 3.5 reduce_sum.65
  624.7 2.2 fusion.6
  (52 shorter events, 1.3 us)
Async XLA Ops:
  7.2 10.5 %copy-start = (s32[1,1,8]{2,1,0:T(1,128)S(1)}, s32[1,1,8]{2,1,0:T(1,128)}, u32[]{:S(2)}) copy-start(s32[1,1,8]{2,1,0:T(1,128)} %param.12) | copy-start | bytes 100
  7.2 13.4 %copy-start.2 = (bf16[1,1,256,1024]{3,2,1,0:T(8,128)(2,1)S(1)}, bf16[1,1,256,1024]{3,2,1,0:T(8,128)(2,1)}, u32[]{:S(2)}) copy-start(bf16[1,1,256,1024]{3,2,1,0:T(8,128)(2,1)} %param.10) | copy-start | bytes 1572868
  7.2 13.4 %copy-start.1 = (f32[1,1,1024,256]{3,2,1,0:T(8,128)S(1)}, f32[1,1,1024,256]{3,2,1,0:T(8,128)}, u32[]{:S(2)}) copy-start(f32[1,1,1024,256]{3,2,1,0:T(8,128)} %param.9) | copy-start | bytes 3145732
  11.8 28.2 %all-to-all-start = ((s32[8,2,1]{1,2,0:T(1,128)}), s32[8,2,1]{1,2,0:T(1,128)S(1)}, u32[]{:S(2)}, u32[]{:S(2)}) async-start(s32[8,2,1]{1,2,0:T(1,128)} %bitcast.9), calls=%async_computation | async-start | bytes 8192 | tf_op jit(solution)/shard_map/all_to_all | solution.py:79
  20.5 17.8 %copy-start.4 = (bf16[1,1,8,32,1024]{4,3,2,1,0:T(8,128)(2,1)S(1)}, bf16[1,1,8,32,1024]{4,3,2,1,0:T(8,128)(2,1)}, u32[]{:S(2)}) copy-start(bf16[1,1,8,32,1024]{4,3,2,1,0:T(8,128)(2,1)} %param.11) | copy-start | bytes 1572868
  40.0 10.7 %all-to-all-start.1 = ((bf16[16,32,256]{2,1,0:T(8,128)(2,1)}), bf16[16,32,256]{2,1,0:T(8,128)(2,1)S(1)}, u32[]{:S(2)}, u32[]{:S(2)}) async-start(bf16[16,32,256]{2,1,0:T(8,128)(2,1)} %broadcast_select_fusion.3), calls=%async_computation.1 | async-start | bytes 524288 | tf_op jit(solution)/shard_map/all_to_all | solution.py:78
  43.8 124.6 %all-gather.5.cloned.1.call-start = ((), (), s32[]{:S(2)}) async-start(), calls=%async_computation.8 | async-start | bytes 7864320 | tf_op jit(solution)/shard_map/all_gather | solution.py:90
  53.3 140.3 %all-to-all-start.2 = ((s32[8,2,1]{1,2,0:T(1,128)}), s32[8,2,1]{1,2,0:T(1,128)S(1)}, u32[]{:S(2)}, u32[]{:S(2)}) async-start(s32[8,2,1]{1,2,0:T(1,128)} %bitcast.20), calls=%async_computation.2 | async-start | bytes 8192 | tf_op jit(solution)/shard_map/all_to_all | solution.py:79
  193.6 10.6 %all-to-all-start.3 = ((bf16[16,32,256]{2,1,0:T(8,128)(2,1)}), bf16[16,32,256]{2,1,0:T(8,128)(2,1)S(1)}, u32[]{:S(2)}, u32[]{:S(2)}) async-start(bf16[16,32,256]{2,1,0:T(8,128)(2,1)} %broadcast_select_fusion.2), calls=%async_computation.3 | async-start | bytes 524288 | tf_op jit(solution)/shard_map/all_to_all | solution.py:78
  197.2 121.5 %all-gather.7.cloned.1.call-start = ((), (), s32[]{:S(2)}) async-start(), calls=%async_computation.9 | async-start | bytes 7864320 | tf_op jit(solution)/shard_map/all_gather | solution.py:90
  206.7 138.7 %all-to-all-start.4 = ((s32[8,2,1]{1,2,0:T(1,128)}), s32[8,2,1]{1,2,0:T(1,128)S(1)}, u32[]{:S(2)}, u32[]{:S(2)}) async-start(s32[8,2,1]{1,2,0:T(1,128)} %bitcast.24), calls=%async_computation.4 | async-start | bytes 8192 | tf_op jit(solution)/shard_map/all_to_all | solution.py:79
  345.4 10.6 %all-to-all-start.5 = ((bf16[16,32,256]{2,1,0:T(8,128)(2,1)}), bf16[16,32,256]{2,1,0:T(8,128)(2,1)S(1)}, u32[]{:S(2)}, u32[]{:S(2)}) async-start(bf16[16,32,256]{2,1,0:T(8,128)(2,1)} %broadcast_select_fusion.1), calls=%async_computation.5 | async-start | bytes 524288 | tf_op jit(solution)/shard_map/all_to_all | solution.py:78
  349.0 121.6 %all-gather.9.cloned.1.call-start = ((), (), s32[]{:S(2)}) async-start(), calls=%async_computation.10 | async-start | bytes 7864320 | tf_op jit(solution)/shard_map/all_gather | solution.py:90
  358.6 137.6 %all-to-all-start.6 = ((s32[8,2,1]{1,2,0:T(1,128)}), s32[8,2,1]{1,2,0:T(1,128)S(1)}, u32[]{:S(2)}, u32[]{:S(2)}) async-start(s32[8,2,1]{1,2,0:T(1,128)} %bitcast.29), calls=%async_computation.6 | async-start | bytes 8192 | tf_op jit(solution)/shard_map/all_to_all | solution.py:79
  361.9 113.3 %copy-start.3 = (f32[256,256]{1,0:T(8,128)S(1)}, f32[256,256]{1,0:T(8,128)}, u32[]{:S(2)}) copy-start(f32[256,256]{1,0:T(8,128)} %get-tuple-element.25) | copy-start | bytes 786436
  496.2 10.5 %all-to-all-start.7 = ((bf16[16,32,256]{2,1,0:T(8,128)(2,1)}), bf16[16,32,256]{2,1,0:T(8,128)(2,1)S(1)}, u32[]{:S(2)}, u32[]{:S(2)}) async-start(bf16[16,32,256]{2,1,0:T(8,128)(2,1)} %broadcast_select_fusion), calls=%async_computation.7 | async-start | bytes 524288 | tf_op jit(solution)/shard_map/all_to_all | solution.py:78
  499.7 121.5 %all-gather.11.cloned.1.call-start = ((), (), s32[]{:S(2)}) async-start(), calls=%async_computation.11 | async-start | bytes 7864320 | tf_op jit(solution)/shard_map/all_gather | solution.py:90
Sparse Core Ops, SparseCore 0:
  53.4 114.9 all-gather.4
  206.8 111.8 all-gather.6
  358.7 111.8 all-gather.8
  509.4 111.8 all-gather.10
